TPU v7x, 512 devices: a whole 4x8x8 slice. The times are simulated.
512 devices in a mesh: seq: 64 (over z, y), chan: 8 (over x, core).
Axes of the slice: x: 4, y: 8, z: 8, core: 2. Of those that a mesh axis runs over, the one named last changes fastest.
Arguments:
- tokens: bfloat16 [8192, 4096], P('seq', 'chan'), may hold values from -6 to 6
- conv_taps: float32 [4, 4096], P(None, 'chan'), may hold values from -12 to 12
- log_rate: float32 [4096], P('chan'), may hold values from 4.8828125e-06 to 0.034
- rotation: float32 [4096], P('chan'), may hold values from 0 to 0.2
- in_proj: bfloat16 [64, 64, 128], P('chan'), may hold values from -0.75 to 0.75
- out_proj: bfloat16 [64, 64, 128], P('chan'), may hold values from -0.5 to 0.5
- skip_gain: float32 [4096], P('chan'), may hold values from 0.25 to 1.5
- norm_gain: float32 [4096], P('chan'), may hold values from 0.25 to 1.75
- retention: float32 [8192], P('seq'), may hold values from 0.5 to 1
- cotangent: bfloat16 [8192, 4096], P('seq', 'chan'), may hold values from -6 to 6
Outputs:
- normed: bfloat16 [8192, 4096], P('seq', 'chan')
- tokens_grad: bfloat16 [8192, 4096], P('seq', 'chan')
- in_grad: float32 [64, 64, 128], P('chan')
- out_grad: float32 [64, 64, 128], P('chan')
- taps_grad: float32 [4, 4096], P(None, 'chan')
All inputs are finite; a program needn't handle non-finite values.
Results may differ from a plain program's by a relative error of at most 0.011.
Values may be sent and summed in bfloat16 or wider, within the bound.
No kernel may reach another device: no remote copies, remote signals or barrier semaphores. Data moves between devices by JAX's collectives and lax.ppermute only.
A program may use at most 64 MiB of HBM per device.

v0:
```python
import jax
import jax.numpy as jnp
from jax import lax
from jax.sharding import Mesh, PartitionSpec as P

SEQ = ("z", "y")


def from_behind(value, axis, by):
    length = lax.axis_size(axis)
    pairs = [(i, i + by) for i in range(length) if 0 <= i + by < length]
    return lax.ppermute(value, axis, pairs)


def carried_in(part, axis, combine, identity, reverse):
    count = lax.axis_size(axis)
    place = lax.axis_index(axis)
    ahead = count - 1 - place if reverse else place
    step = -1 if reverse else 1
    packed = jnp.stack(part)
    unit = jnp.stack([jnp.zeros_like(a) + jnp.asarray(e, a.dtype) for a, e in zip(part, identity)])
    state = jnp.where(ahead >= 1, from_behind(packed, axis, step), unit)
    reach = 1
    while reach < count:
        earlier = from_behind(state, axis, step * reach)
        joined = jnp.stack(combine(tuple(earlier), tuple(state)))
        state = jnp.where(ahead >= reach, joined, state)
        reach *= 2
    return tuple(state)


def linear_run(drive_re, drive_im, decay_rate, turn_rate, log_keep):
    seq_len, num_cols = drive_re.shape
    block_len = min(64, seq_len)
    block_count = seq_len // block_len
    offsets = jnp.arange(block_len, dtype=jnp.float32)
    keep_cum = jnp.cumsum(log_keep.reshape(block_count, block_len), axis=1)[:, :, None]
    angles = offsets[:, None] * turn_rate[None, :]
    cosine = jnp.cos(angles)
    sine = jnp.sin(angles)
    growth = jnp.exp(offsets[None, :, None] * decay_rate[None, None, :] - keep_cum)
    blk_re = drive_re.reshape(block_count, block_len, num_cols)
    blk_im = drive_im.reshape(block_count, block_len, num_cols)
    pre_re = growth * (blk_re * cosine + blk_im * sine)
    pre_im = growth * (blk_im * cosine - blk_re * sine)
    lower_ones = (offsets[:, None] >= offsets[None, :]).astype(jnp.float32)
    summed = jnp.einsum(
        "ji,abik->abjk", lower_ones, jnp.stack([pre_re, pre_im]), precision=lax.Precision.HIGHEST
    )
    shrink = jnp.exp(keep_cum - offsets[None, :, None] * decay_rate[None, None, :])
    state_re = shrink * (summed[0] * cosine - summed[1] * sine)
    state_im = shrink * (summed[0] * sine + summed[1] * cosine)
    step_mag = jnp.exp(keep_cum[:, -1] - block_len * decay_rate[None, :])
    step_re = step_mag * jnp.cos(block_len * turn_rate)[None, :]
    step_im = step_mag * jnp.sin(block_len * turn_rate)[None, :]

    def advance(carried, inputs):
        carry_re, carry_im = carried
        mult_re, mult_im, end_re, end_im = inputs
        next_re = mult_re * carry_re - mult_im * carry_im + end_re
        next_im = mult_re * carry_im + mult_im * carry_re + end_im
        return ((next_re, next_im), (carry_re, carry_im))

    zeros_col = jnp.zeros((num_cols,), jnp.float32)
    enter_re, enter_im = lax.scan(
        advance, (zeros_col, zeros_col), (step_re, step_im, state_re[:, -1], state_im[:, -1])
    )[1]
    ahead = offsets + 1.0
    lift = jnp.exp(keep_cum - ahead[None, :, None] * decay_rate[None, None, :])
    lift_re = lift * jnp.cos(ahead[:, None] * turn_rate[None, :])
    lift_im = lift * jnp.sin(ahead[:, None] * turn_rate[None, :])
    state_re = state_re + lift_re * enter_re[:, None] - lift_im * enter_im[:, None]
    state_im = state_im + lift_re * enter_im[:, None] + lift_im * enter_re[:, None]
    return (state_re.reshape(seq_len, num_cols), state_im.reshape(seq_len, num_cols))


def carry_combine(earlier, later):
    early_re, early_im, early_sre, early_sim = earlier
    late_re, late_im, late_sre, late_sim = later
    joined_re = early_re * late_re - early_im * late_im
    joined_im = early_re * late_im + early_im * late_re
    joined_sre = late_re * early_sre - late_im * early_sim + late_sre
    joined_sim = late_re * early_sim + late_im * early_sre + late_sim
    return (joined_re, joined_im, joined_sre, joined_sim)


def per_device(
    tokens,
    conv_taps,
    log_rate,
    rotation,
    in_proj,
    out_proj,
    skip_gain,
    norm_gain,
    retention,
    cotangent,
):
    seq_len, local_width = tokens.shape
    tap_count = conv_taps.shape[0]
    local_heads, head_width, double_state = in_proj.shape
    state_size = double_state // 2
    num_cols = local_heads * state_size
    lead_rows = from_behind(tokens[seq_len - (tap_count - 1) :], SEQ, 1)
    padded = jnp.concatenate([lead_rows, tokens], axis=0).astype(jnp.float32)
    conv_sum = conv_taps[0][None, :] * padded[tap_count - 1 :]
    for offset in range(1, tap_count):
        conv_sum = (
            conv_sum
            + conv_taps[offset][None, :]
            * padded[tap_count - 1 - offset : tap_count - 1 - offset + seq_len]
        )
    mixed_in = conv_sum.astype(jnp.bfloat16)
    by_head = mixed_in.reshape(seq_len, local_heads, head_width)
    projected = jnp.einsum("thc,hck->thk", by_head, in_proj, preferred_element_type=jnp.float32)
    in_scale = jnp.sqrt(-jnp.expm1(-2.0 * log_rate))
    drive_re = projected[:, :, :state_size].reshape(seq_len, num_cols) * in_scale
    drive_im = projected[:, :, state_size:].reshape(seq_len, num_cols) * in_scale
    log_keep = jnp.log(retention)
    state_re, state_im = linear_run(drive_re, drive_im, log_rate, rotation, log_keep)
    keep_total = jnp.sum(log_keep)
    total_mag = jnp.exp(keep_total - seq_len * log_rate)
    total_re = total_mag * jnp.cos(seq_len * rotation)
    total_im = total_mag * jnp.sin(seq_len * rotation)
    unit_ones = jnp.ones((num_cols,), jnp.float32)
    zeros_col = jnp.zeros((num_cols,), jnp.float32)
    chained = carried_in(
        (total_re, total_im, state_re[-1], state_im[-1]),
        SEQ,
        carry_combine,
        (unit_ones, zeros_col, zeros_col, zeros_col),
        False,
    )
    enter_re, enter_im = (chained[2], chained[3])
    positions = jnp.arange(seq_len, dtype=jnp.float32)
    ahead = positions + 1.0
    lift = jnp.exp(jnp.cumsum(log_keep)[:, None] - ahead[:, None] * log_rate[None, :])
    lift_re = lift * jnp.cos(ahead[:, None] * rotation[None, :])
    lift_im = lift * jnp.sin(ahead[:, None] * rotation[None, :])
    state_re = state_re + lift_re * enter_re[None, :] - lift_im * enter_im[None, :]
    state_im = state_im + lift_re * enter_im[None, :] + lift_im * enter_re[None, :]
    state_bf = jnp.concatenate(
        [
            state_re.reshape(seq_len, local_heads, state_size),
            state_im.reshape(seq_len, local_heads, state_size),
        ],
        axis=2,
    ).astype(jnp.bfloat16)
    mixed = jnp.einsum(
        "thk,hck->thc", state_bf, out_proj, preferred_element_type=jnp.float32
    ).reshape(seq_len, local_width)
    mixed = mixed + skip_gain * mixed_in.astype(jnp.float32)
    squares = jnp.sum(mixed * mixed, axis=1)
    scaled = cotangent.astype(jnp.float32) * norm_gain
    dots = jnp.sum(scaled * mixed, axis=1)
    squares = lax.psum(squares, "chan")
    model_width = local_width * lax.axis_size("chan")
    inverse = lax.rsqrt(squares / model_width + 1e-06)
    normed = (mixed * inverse[:, None] * norm_gain).astype(jnp.bfloat16)
    dots = lax.psum(dots, "chan")
    mixed_grad = inverse[:, None] * (
        scaled - mixed * (inverse * inverse * dots / model_width)[:, None]
    )
    grad_bf = mixed_grad.astype(jnp.bfloat16).reshape(seq_len, local_heads, head_width)
    state_grad = jnp.einsum("thc,hck->thk", grad_bf, out_proj, preferred_element_type=jnp.float32)
    out_grad = jnp.einsum("thc,thk->hck", grad_bf, state_bf, preferred_element_type=jnp.float32)
    out_grad = lax.psum(lax.psum(out_grad, "y"), "z")
    back_keep = jnp.concatenate([jnp.zeros((1,), jnp.float32), log_keep[::-1][:-1]])
    grad_re = state_grad[:, :, :state_size].reshape(seq_len, num_cols)[::-1]
    grad_im = state_grad[:, :, state_size:].reshape(seq_len, num_cols)[::-1]
    adj_re, adj_im = linear_run(grad_re, grad_im, log_rate, -rotation, back_keep)
    first_mag = jnp.exp(log_keep[0] - log_rate)
    cos_turn = jnp.cos(rotation)
    sin_turn = jnp.sin(rotation)
    first_re = first_mag * (cos_turn * adj_re[-1] + sin_turn * adj_im[-1])
    first_im = first_mag * (cos_turn * adj_im[-1] - sin_turn * adj_re[-1])
    back_chained = carried_in(
        (total_re, -total_im, first_re, first_im),
        SEQ,
        carry_combine,
        (unit_ones, zeros_col, zeros_col, zeros_col),
        True,
    )
    later_re, later_im = (back_chained[2], back_chained[3])
    back_lift = jnp.exp(jnp.cumsum(back_keep)[:, None] - positions[:, None] * log_rate[None, :])
    back_re = back_lift * jnp.cos(positions[:, None] * rotation[None, :])
    back_im = -back_lift * jnp.sin(positions[:, None] * rotation[None, :])
    adj_re = adj_re + back_re * later_re[None, :] - back_im * later_im[None, :]
    adj_im = adj_im + back_re * later_im[None, :] + back_im * later_re[None, :]
    adj_re = adj_re[::-1]
    adj_im = adj_im[::-1]
    drive_grad = jnp.concatenate(
        [
            (in_scale * adj_re).reshape(seq_len, local_heads, state_size),
            (in_scale * adj_im).reshape(seq_len, local_heads, state_size),
        ],
        axis=2,
    ).astype(jnp.bfloat16)
    in_grad = jnp.einsum("thc,thk->hck", by_head, drive_grad, preferred_element_type=jnp.float32)
    input_grad = jnp.einsum(
        "thk,hck->thc", drive_grad, in_proj, preferred_element_type=jnp.float32
    ).reshape(seq_len, local_width)
    input_grad = input_grad + skip_gain * mixed_grad
    trail_rows = from_behind(input_grad[: tap_count - 1], SEQ, -1)
    tail = jnp.concatenate([input_grad, trail_rows], axis=0)
    tokens_grad = conv_taps[0][None, :] * tail[:seq_len]
    for offset in range(1, tap_count):
        tokens_grad = tokens_grad + conv_taps[offset][None, :] * tail[offset : offset + seq_len]
    taps_grad = jnp.stack(
        [
            jnp.sum(
                input_grad * padded[tap_count - 1 - offset : tap_count - 1 - offset + seq_len],
                axis=0,
            )
            for offset in range(tap_count)
        ]
    )
    packed = jnp.concatenate([in_grad.reshape(-1), taps_grad.reshape(-1)])
    packed = lax.psum(lax.psum(packed, "y"), "z")
    in_grad = packed[: in_grad.size].reshape(in_grad.shape)
    taps_grad = packed[in_grad.size :].reshape(taps_grad.shape)
    return (normed, tokens_grad.astype(jnp.bfloat16), in_grad, out_grad, taps_grad)


def solution(mesh):
    seq_count, chan_count = mesh.devices.shape
    inner = 1
    while inner * inner < seq_count:
        inner *= 2
    devices = mesh.devices.reshape(seq_count // inner, inner, chan_count)
    mesh = Mesh(devices, SEQ + ("chan",))
    in_specs = (
        P(SEQ, "chan"),
        P(None, "chan"),
        P("chan"),
        P("chan"),
        P("chan", None, None),
        P("chan", None, None),
        P("chan"),
        P("chan"),
        P(SEQ),
        P(SEQ, "chan"),
    )
    out_specs = (
        P(SEQ, "chan"),
        P(SEQ, "chan"),
        P("chan", None, None),
        P("chan", None, None),
        P(None, "chan"),
    )
    return jax.shard_map(
        per_device, mesh=mesh, in_specs=in_specs, out_specs=out_specs, check_vma=False
    )
```

profile of v0, /device:TPU:2, one launch (start us, length us, event | category | flops | bytes accessed | tf_op | source)
XLA Modules:
  0.0 364.7 jit_solution(13326804845153230500)
XLA Ops:
  8.2 3.5 collective-permute-start
  14.9 1.3 fusion.68
  16.2 2.5 multiply_cosine_fusion.1
  21.0 1.0 fusion.18
  27.2 3.5 collective-permute-start.1
  30.7 1.3 collective-permute-done.1
  32.1 4.2 %collective-permute-start.2 = (f32[4,512]{1,0:T(4,128)S(1)}, f32[4,512]{1,0:T(4,128)S(1)}, u32[]{:S(2)}, u32[]{:S(2)}) collective-permute-start(f32[4,512]{1,0:T(4,128)S(1)} %broadcast_select_fusion.5), channel_id=1, source_target_pairs={{0,8},{8,16},{16,24},{24,32},{32,40},{40,48},{48,56},{56,64},{64,7... | collective-permute-start | bytes 24584 | tf_op jit(solution)/shard_map/ppermute | solution.py:12
  36.2 1.3 collective-permute-done.2
  37.6 5.7 %collective-permute-start.3 = (f32[4,512]{1,0:T(4,128)S(1)}, f32[4,512]{1,0:T(4,128)S(1)}, u32[]{:S(2)}, u32[]{:S(2)}) collective-permute-start(f32[4,512]{1,0:T(4,128)S(1)} %maximum_select_fusion), channel_id=1, source_target_pairs={{0,16},{8,24},{16,32},{24,40},{32,48},{40,56},{48,64},{56,72},{64,... | collective-permute-start | bytes 24584 | tf_op jit(solution)/shard_map/ppermute | solution.py:12
  43.4 1.3 collective-permute-done.3
  44.8 10.6 %collective-permute-start.4 = (f32[4,512]{1,0:T(4,128)S(1)}, f32[4,512]{1,0:T(4,128)S(1)}, u32[]{:S(2)}, u32[]{:S(2)}) collective-permute-start(f32[4,512]{1,0:T(4,128)S(1)} %maximum_select_fusion.1), channel_id=1, source_target_pairs={{0,32},{8,40},{16,48},{24,56},{32,64},{40,72},{48,80},{56,88},{64,... | collective-permute-start | bytes 24584 | tf_op jit(solution)/shard_map/ppermute | solution.py:12
  55.4 1.3 collective-permute-done.4
  56.8 9.1 %collective-permute-start.5 = (f32[4,512]{1,0:T(4,128)S(1)}, f32[4,512]{1,0:T(4,128)S(1)}, u32[]{:S(2)}, u32[]{:S(2)}) collective-permute-start(f32[4,512]{1,0:T(4,128)S(1)} %maximum_select_fusion.2), channel_id=1, source_target_pairs={{0,64},{8,72},{16,80},{24,88},{32,96},{40,104},{48,112},{56,120},{... | collective-permute-start | bytes 24584 | tf_op jit(solution)/shard_map/ppermute | solution.py:12
  65.9 1.3 collective-permute-done.5
  67.4 6.1 %collective-permute-start.6 = (f32[4,512]{1,0:T(4,128)S(1)}, f32[4,512]{1,0:T(4,128)S(1)}, u32[]{:S(2)}, u32[]{:S(2)}) collective-permute-start(f32[4,512]{1,0:T(4,128)S(1)} %maximum_select_fusion.3), channel_id=1, source_target_pairs={{0,128},{8,136},{16,144},{24,152},{32,160},{40,168},{48,176},{56,1... | collective-permute-start | bytes 24584 | tf_op jit(solution)/shard_map/ppermute | solution.py:12
  73.5 1.3 collective-permute-done.6
  76.1 17.7 %collective-permute-start.7 = (f32[4,512]{1,0:T(4,128)}, f32[4,512]{1,0:T(4,128)}, u32[]{:S(2)}, u32[]{:S(2)}) collective-permute-start(f32[4,512]{1,0:T(4,128)} %maximum_select_fusion.4), channel_id=1, source_target_pairs={{0,256},{8,264},{16,272},{24,280},{32,288},{40,296},{48,304},{56,3... | collective-permute-start | bytes 24584 | tf_op jit(solution)/shard_map/ppermute | solution.py:12
  97.4 1.1 sub.357
  99.4 0.9 copy.136
  100.3 0.9 copy.138
  102.5 0.9 copy.140
  108.8 1.1 squeeze.79
  109.9 0.9 copy.141
  111.7 0.9 copy.135
  113.0 0.9 multiply_subtract_fusion.7
  115.5 2.7 subtract_convert_fusion
  119.7 10.2 %all-reduce = (f32[128]{0:T(128)S(1)}, f32[128]{0:T(128)S(1)}) all-reduce(f32[128]{0:T(128)S(1)} %get-tuple-element.185, f32[128]{0:T(128)S(1)} %get-tuple-element.184), channel_id=1, replica_groups=mesh['z'=8,'y'=8,'chan'=8] {'chan'}, use_global_device_ids=true, to_apply=%region_6.7 | all-reduce | flops 256 | bytes 2048 | tf_op jit(solution)/shard_map/psum | solution.py:156
  137.2 1.3 collective-permute-start.8
  138.5 4.2 %collective-permute-done.8 = f32[4,512]{1,0:T(4,128)S(1)} collective-permute-done((f32[4,512]{1,0:T(4,128)S(1)}, f32[4,512]{1,0:T(4,128)S(1)}, u32[]{:S(2)}, u32[]{:S(2)}) %collective-permute-start.8) | collective-permute-done | bytes 8224 | tf_op jit(solution)/shard_map/ppermute | solution.py:12
  142.7 1.3 collective-permute-start.9
  144.0 4.2 %collective-permute-done.9 = f32[4,512]{1,0:T(4,128)S(1)} collective-permute-done((f32[4,512]{1,0:T(4,128)S(1)}, f32[4,512]{1,0:T(4,128)S(1)}, u32[]{:S(2)}, u32[]{:S(2)}) %collective-permute-start.9) | collective-permute-done | bytes 8224 | tf_op jit(solution)/shard_map/ppermute | solution.py:12
  148.3 1.3 collective-permute-start.10
  149.6 5.1 %collective-permute-done.10 = f32[4,512]{1,0:T(4,128)S(1)} collective-permute-done((f32[4,512]{1,0:T(4,128)S(1)}, f32[4,512]{1,0:T(4,128)S(1)}, u32[]{:S(2)}, u32[]{:S(2)}) %collective-permute-start.10) | collective-permute-done | bytes 8224 | tf_op jit(solution)/shard_map/ppermute | solution.py:12
  154.8 1.3 collective-permute-start.11
  156.1 8.1 %collective-permute-done.11 = f32[4,512]{1,0:T(4,128)S(1)} collective-permute-done((f32[4,512]{1,0:T(4,128)S(1)}, f32[4,512]{1,0:T(4,128)S(1)}, u32[]{:S(2)}, u32[]{:S(2)}) %collective-permute-start.11) | collective-permute-done | bytes 8224 | tf_op jit(solution)/shard_map/ppermute | solution.py:12
  164.3 1.3 collective-permute-start.12
  165.6 4.3 %collective-permute-done.12 = f32[4,512]{1,0:T(4,128)S(1)} collective-permute-done((f32[4,512]{1,0:T(4,128)S(1)}, f32[4,512]{1,0:T(4,128)S(1)}, u32[]{:S(2)}, u32[]{:S(2)}) %collective-permute-start.12) | collective-permute-done | bytes 8224 | tf_op jit(solution)/shard_map/ppermute | solution.py:12
  170.0 1.3 collective-permute-start.13
  172.3 4.1 %collective-permute-done.13 = f32[4,512]{1,0:T(4,128)S(1)} collective-permute-done((f32[4,512]{1,0:T(4,128)S(1)}, f32[4,512]{1,0:T(4,128)S(1)}, u32[]{:S(2)}, u32[]{:S(2)}) %collective-permute-start.13) | collective-permute-done | bytes 8224 | tf_op jit(solution)/shard_map/ppermute | solution.py:12
  176.5 1.3 collective-permute-start.14
  177.8 1.0 fusion.35
  178.8 7.2 %collective-permute-done.14 = f32[4,512]{1,0:T(4,128)S(1)} collective-permute-done((f32[4,512]{1,0:T(4,128)S(1)}, f32[4,512]{1,0:T(4,128)S(1)}, u32[]{:S(2)}, u32[]{:S(2)}) %collective-permute-start.14) | collective-permute-done | bytes 8224 | tf_op jit(solution)/shard_map/ppermute | solution.py:12
  186.7 1.1 multiply_subtract_fusion
  192.1 80.6 %all-reduce.6.cloned.1.call-done = (f32[67584]{0:T(1024)}, f32[8,64,128]{2,1,0:T(8,128)}) async-done(((f32[67584]{0:T(1024)}, f32[8,64,128]{2,1,0:T(8,128)}), (f32[67584]{0:T(1024)}, f32[8,64,128]{2,1,0:T(8,128)})) %all-reduce.6.cloned.1.call-update) | async-done | bytes 532496 | tf_op jit(solution)/shard_map/psum | solution.py:219
  272.7 1.3 collective-permute-start.15
  274.8 6.2 %collective-permute-done.15 = f32[3,512]{0,1:T(8,128)S(1)} collective-permute-done((f32[3,512]{0,1:T(8,128)S(1)}, f32[3,512]{0,1:T(8,128)S(1)}, u32[]{:S(2)}, u32[]{:S(2)}) %collective-permute-start.15) | collective-permute-done | bytes 6176 | tf_op jit(solution)/shard_map/ppermute | solution.py:12
  282.5 71.6 %all-reduce.8.cloned.1.call-done = (f32[67584]{0:T(1024)}, f32[8,64,128]{2,1,0:T(8,128)}) async-done(((f32[67584]{0:T(1024)}, f32[8,64,128]{2,1,0:T(8,128)}), (f32[67584]{0:T(1024)}, f32[8,64,128]{2,1,0:T(8,128)})) %all-reduce.8.cloned.1.call-update) | async-done | bytes 532496 | tf_op jit(solution)/shard_map/psum | solution.py:219
  354.1 1.7 slice.228
  (359 shorter events, 45.8 us)
Async XLA Ops:
  7.2 111.1 %copy-start = (bf16[8,64,128]{2,1,0:T(8,128)(2,1)S(1)}, bf16[8,64,128]{2,1,0:T(8,128)(2,1)}, u32[]{:S(2)}) copy-start(bf16[8,64,128]{2,1,0:T(8,128)(2,1)} %param.19) | copy-start | bytes 393220
  7.2 265.5 %all-reduce.6.cloned.1.call-start = ((), (), s32[]{:S(2)}) async-start(), calls=%async_computation | async-start | bytes 1064960 | tf_op jit(solution)/shard_map/psum | solution.py:219
  8.1 3.5 copy-start.88
  8.2 13.9 %collective-permute-start = (bf16[3,512]{0,1:T(8,128)(2,1)S(1)}, bf16[3,512]{0,1:T(8,128)(2,1)S(1)}, u32[]{:S(2)}, u32[]{:S(2)}) collective-permute-start(bf16[3,512]{0,1:T(8,128)(2,1)S(1)} %copy.131), channel_id=1, source_target_pairs={{0,8},{8,16},{16,24},{24,32},{32,40},{40,48},{48,56},{56,64},{64,7... | collective-permute-start | bytes 9224 | tf_op jit(solution)/shard_map/ppermute | solution.py:12
  14.2 81.8 %copy-start.72 = (f32[2,64]{1,0:T(2,128)}, f32[2,64]{1,0:T(2,128)S(1)}, u32[]{:S(2)}) copy-start(f32[2,64]{1,0:T(2,128)S(1)} %reduce.6) | copy-start | bytes 1540
  16.2 8.3 %copy-start.57 = (f32[512]{0:T(512)}, f32[512]{0:T(512)S(1)}, u32[]{:S(2)}) copy-start(f32[512]{0:T(512)S(1)} %get-tuple-element.356) | copy-start | bytes 6148
  16.2 11.0 %copy-start.59 = (f32[512]{0:T(512)}, f32[512]{0:T(512)S(1)}, u32[]{:S(2)}) copy-start(f32[512]{0:T(512)S(1)} %get-tuple-element.352) | copy-start | bytes 6148
  18.7 1.5 copy-start.14
  20.2 2.0 copy-start.49
  20.3 2.0 copy-start.51
  20.3 2.0 copy-start.53
  20.3 2.0 copy-start.55
  27.2 4.8 %collective-permute-start.1 = (f32[4,512]{1,0:T(4,128)S(1)}, f32[4,512]{1,0:T(4,128)S(1)}, u32[]{:S(2)}, u32[]{:S(2)}) collective-permute-start(f32[4,512]{1,0:T(4,128)S(1)} %fusion.48), channel_id=1, source_target_pairs={{0,8},{8,16},{16,24},{24,32},{32,40},{40,48},{48,56},{56,64},{64,7... | collective-permute-start | bytes 24584 | tf_op jit(solution)/shard_map/ppermute | solution.py:12
  32.1 5.5 %collective-permute-start.2 = (f32[4,512]{1,0:T(4,128)S(1)}, f32[4,512]{1,0:T(4,128)S(1)}, u32[]{:S(2)}, u32[]{:S(2)}) collective-permute-start(f32[4,512]{1,0:T(4,128)S(1)} %broadcast_select_fusion.5), channel_id=1, source_target_pairs={{0,8},{8,16},{16,24},{24,32},{32,40},{40,48},{48,56},{56,64},{64,7... | collective-permute-start | bytes 24584 | tf_op jit(solution)/shard_map/ppermute | solution.py:12
  37.6 7.1 %collective-permute-start.3 = (f32[4,512]{1,0:T(4,128)S(1)}, f32[4,512]{1,0:T(4,128)S(1)}, u32[]{:S(2)}, u32[]{:S(2)}) collective-permute-start(f32[4,512]{1,0:T(4,128)S(1)} %maximum_select_fusion), channel_id=1, source_target_pairs={{0,16},{8,24},{16,32},{24,40},{32,48},{40,56},{48,64},{56,72},{64,... | collective-permute-start | bytes 24584 | tf_op jit(solution)/shard_map/ppermute | solution.py:12
  44.7 30.2 %copy-start.17 = (f32[1,512]{1,0:T(1,128)}, f32[1,512]{1,0:T(1,128)S(1)}, u32[]{:S(2)}) copy-start(f32[1,512]{1,0:T(1,128)S(1)} %get-tuple-element.319) | copy-start | bytes 6148
  44.7 30.2 %copy-start.19 = (f32[1,512]{1,0:T(1,128)}, f32[1,512]{1,0:T(1,128)S(1)}, u32[]{:S(2)}) copy-start(f32[1,512]{1,0:T(1,128)S(1)} %get-tuple-element.320) | copy-start | bytes 6148
  44.7 30.2 %copy-start.21 = (f32[1,512]{1,0:T(1,128)}, f32[1,512]{1,0:T(1,128)S(1)}, u32[]{:S(2)}) copy-start(f32[1,512]{1,0:T(1,128)S(1)} %get-tuple-element.321) | copy-start | bytes 6148
  44.8 30.2 %copy-start.23 = (f32[1,512]{1,0:T(1,128)}, f32[1,512]{1,0:T(1,128)S(1)}, u32[]{:S(2)}) copy-start(f32[1,512]{1,0:T(1,128)S(1)} %get-tuple-element.322) | copy-start | bytes 6148
  44.8 11.9 %collective-permute-start.4 = (f32[4,512]{1,0:T(4,128)S(1)}, f32[4,512]{1,0:T(4,128)S(1)}, u32[]{:S(2)}, u32[]{:S(2)}) collective-permute-start(f32[4,512]{1,0:T(4,128)S(1)} %maximum_select_fusion.1), channel_id=1, source_target_pairs={{0,32},{8,40},{16,48},{24,56},{32,64},{40,72},{48,80},{56,88},{64,... | collective-permute-start | bytes 24584 | tf_op jit(solution)/shard_map/ppermute | solution.py:12
  56.7 18.2 %copy-start.29 = (f32[1,512]{1,0:T(1,128)}, f32[1,512]{1,0:T(1,128)S(1)}, u32[]{:S(2)}) copy-start(f32[1,512]{1,0:T(1,128)S(1)} %get-tuple-element.315) | copy-start | bytes 6148
  56.7 18.2 %copy-start.31 = (f32[1,512]{1,0:T(1,128)}, f32[1,512]{1,0:T(1,128)S(1)}, u32[]{:S(2)}) copy-start(f32[1,512]{1,0:T(1,128)S(1)} %get-tuple-element.316) | copy-start | bytes 6148
  56.7 18.2 %copy-start.33 = (f32[1,512]{1,0:T(1,128)}, f32[1,512]{1,0:T(1,128)S(1)}, u32[]{:S(2)}) copy-start(f32[1,512]{1,0:T(1,128)S(1)} %get-tuple-element.317) | copy-start | bytes 6148
  56.8 18.2 %copy-start.35 = (f32[1,512]{1,0:T(1,128)}, f32[1,512]{1,0:T(1,128)S(1)}, u32[]{:S(2)}) copy-start(f32[1,512]{1,0:T(1,128)S(1)} %get-tuple-element.318) | copy-start | bytes 6148
  56.8 10.5 %collective-permute-start.5 = (f32[4,512]{1,0:T(4,128)S(1)}, f32[4,512]{1,0:T(4,128)S(1)}, u32[]{:S(2)}, u32[]{:S(2)}) collective-permute-start(f32[4,512]{1,0:T(4,128)S(1)} %maximum_select_fusion.2), channel_id=1, source_target_pairs={{0,64},{8,72},{16,80},{24,88},{32,96},{40,104},{48,112},{56,120},{... | collective-permute-start | bytes 24584 | tf_op jit(solution)/shard_map/ppermute | solution.py:12
  67.3 7.7 %copy-start.41 = (f32[1,512]{1,0:T(1,128)}, f32[1,512]{1,0:T(1,128)S(1)}, u32[]{:S(2)}) copy-start(f32[1,512]{1,0:T(1,128)S(1)} %get-tuple-element.311) | copy-start | bytes 6148
  67.3 7.7 %copy-start.43 = (f32[1,512]{1,0:T(1,128)}, f32[1,512]{1,0:T(1,128)S(1)}, u32[]{:S(2)}) copy-start(f32[1,512]{1,0:T(1,128)S(1)} %get-tuple-element.312) | copy-start | bytes 6148
  67.3 7.7 %copy-start.45 = (f32[1,512]{1,0:T(1,128)}, f32[1,512]{1,0:T(1,128)S(1)}, u32[]{:S(2)}) copy-start(f32[1,512]{1,0:T(1,128)S(1)} %get-tuple-element.313) | copy-start | bytes 6148
  67.3 7.7 %copy-start.47 = (f32[1,512]{1,0:T(1,128)}, f32[1,512]{1,0:T(1,128)S(1)}, u32[]{:S(2)}) copy-start(f32[1,512]{1,0:T(1,128)S(1)} %get-tuple-element.314) | copy-start | bytes 6148
  67.4 7.4 %collective-permute-start.6 = (f32[4,512]{1,0:T(4,128)S(1)}, f32[4,512]{1,0:T(4,128)S(1)}, u32[]{:S(2)}, u32[]{:S(2)}) collective-permute-start(f32[4,512]{1,0:T(4,128)S(1)} %maximum_select_fusion.3), channel_id=1, source_target_pairs={{0,128},{8,136},{16,144},{24,152},{32,160},{40,168},{48,176},{56,1... | collective-permute-start | bytes 24584 | tf_op jit(solution)/shard_map/ppermute | solution.py:12
  76.1 36.8 %collective-permute-start.7 = (f32[4,512]{1,0:T(4,128)}, f32[4,512]{1,0:T(4,128)}, u32[]{:S(2)}, u32[]{:S(2)}) collective-permute-start(f32[4,512]{1,0:T(4,128)} %maximum_select_fusion.4), channel_id=1, source_target_pairs={{0,256},{8,264},{16,272},{24,280},{32,288},{40,296},{48,304},{56,3... | collective-permute-start | bytes 24584 | tf_op jit(solution)/shard_map/ppermute | solution.py:12
  111.7 2.2 copy-start.68
  112.6 2.3 copy-start.6
  112.6 2.3 copy-start.7
  112.7 2.3 copy-start.8
  132.1 1.7 copy-start.38
  132.1 2.7 copy-start.11
  132.1 2.7 copy-start.12
  137.2 5.5 %collective-permute-start.8 = (f32[4,512]{1,0:T(4,128)S(1)}, f32[4,512]{1,0:T(4,128)S(1)}, u32[]{:S(2)}, u32[]{:S(2)}) collective-permute-start(f32[4,512]{1,0:T(4,128)S(1)} %fusion.50), channel_id=1, source_target_pairs={{8,0},{16,8},{24,16},{32,24},{40,32},{48,40},{56,48},{64,56},{72,6... | collective-permute-start | bytes 24584 | tf_op jit(solution)/shard_map/ppermute | solution.py:12
  142.7 5.5 %collective-permute-start.9 = (f32[4,512]{1,0:T(4,128)S(1)}, f32[4,512]{1,0:T(4,128)S(1)}, u32[]{:S(2)}, u32[]{:S(2)}) collective-permute-start(f32[4,512]{1,0:T(4,128)S(1)} %broadcast_select_fusion.4), channel_id=1, source_target_pairs={{8,0},{16,8},{24,16},{32,24},{40,32},{48,40},{56,48},{64,56},{72,6... | collective-permute-start | bytes 24584 | tf_op jit(solution)/shard_map/ppermute | solution.py:12
  148.3 6.4 %collective-permute-start.10 = (f32[4,512]{1,0:T(4,128)S(1)}, f32[4,512]{1,0:T(4,128)S(1)}, u32[]{:S(2)}, u32[]{:S(2)}) collective-permute-start(f32[4,512]{1,0:T(4,128)S(1)} %maximum_select_fusion.6), channel_id=1, source_target_pairs={{16,0},{24,8},{32,16},{40,24},{48,32},{56,40},{64,48},{72,56},{80,... | collective-permute-start | bytes 24584 | tf_op jit(solution)/shard_map/ppermute | solution.py:12
  154.8 9.5 %collective-permute-start.11 = (f32[4,512]{1,0:T(4,128)S(1)}, f32[4,512]{1,0:T(4,128)S(1)}, u32[]{:S(2)}, u32[]{:S(2)}) collective-permute-start(f32[4,512]{1,0:T(4,128)S(1)} %maximum_select_fusion.7), channel_id=1, source_target_pairs={{32,0},{40,8},{48,16},{56,24},{64,32},{72,40},{80,48},{88,56},{96,... | collective-permute-start | bytes 24584 | tf_op jit(solution)/shard_map/ppermute | solution.py:12
  164.3 5.6 %collective-permute-start.12 = (f32[4,512]{1,0:T(4,128)S(1)}, f32[4,512]{1,0:T(4,128)S(1)}, u32[]{:S(2)}, u32[]{:S(2)}) collective-permute-start(f32[4,512]{1,0:T(4,128)S(1)} %maximum_select_fusion.8), channel_id=1, source_target_pairs={{64,0},{72,8},{80,16},{88,24},{96,32},{104,40},{112,48},{120,56},{... | collective-permute-start | bytes 24584 | tf_op jit(solution)/shard_map/ppermute | solution.py:12
  170.0 6.4 %collective-permute-start.13 = (f32[4,512]{1,0:T(4,128)S(1)}, f32[4,512]{1,0:T(4,128)S(1)}, u32[]{:S(2)}, u32[]{:S(2)}) collective-permute-start(f32[4,512]{1,0:T(4,128)S(1)} %maximum_select_fusion.9), channel_id=1, source_target_pairs={{128,0},{136,8},{144,16},{152,24},{160,32},{168,40},{176,48},{184,... | collective-permute-start | bytes 24584 | tf_op jit(solution)/shard_map/ppermute | solution.py:12
  176.5 9.5 %collective-permute-start.14 = (f32[4,512]{1,0:T(4,128)S(1)}, f32[4,512]{1,0:T(4,128)S(1)}, u32[]{:S(2)}, u32[]{:S(2)}) collective-permute-start(f32[4,512]{1,0:T(4,128)S(1)} %maximum_select_fusion.10), channel_id=1, source_target_pairs={{256,0},{264,8},{272,16},{280,24},{288,32},{296,40},{304,48},{312,... | collective-permute-start | bytes 24584 | tf_op jit(solution)/shard_map/ppermute | solution.py:12
  192.1 162.0 %all-reduce.8.cloned.1.call-start = ((), (), s32[]{:S(2)}) async-start(), calls=%async_computation.1 | async-start | bytes 1064960 | tf_op jit(solution)/shard_map/psum | solution.py:219
  272.7 8.3 %collective-permute-start.15 = (f32[3,512]{0,1:T(8,128)S(1)}, f32[3,512]{0,1:T(8,128)S(1)}, u32[]{:S(2)}, u32[]{:S(2)}) collective-permute-start(f32[3,512]{0,1:T(8,128)S(1)} %bitcast.248), channel_id=1, source_target_pairs={{8,0},{16,8},{24,16},{32,24},{40,32},{48,40},{56,48},{64,56},{72,6... | collective-permute-start | bytes 18440 | tf_op jit(solution)/shard_map/ppermute | solution.py:12
  354.1 3.0 copy-start.13
  (60 other events, 48.4 us)
Sparse Core Ops, SparseCore 0:
  192.2 80.4 all-reduce.5
  275.1 78.9 all-reduce.7
where the time goes:
time: 366 us; the launch traced here: 365 us
  waiting for transfers between devices  204 us (56%)
  starting transfers between devices  70.7 us (19%)
  local copies, waits for them, and re-layouts  39.3 us (11%)
  other arithmetic  21.6 us (6%)
  between operations  15.8 us (4%)
  blocking collectives  10.2 us (3%)
    psum x2, waiting for transfers between devices, per_device(): packed = lax.psum(lax.psum(packed, 'y'), 'z')  152 us
    ppermute x16, starting transfers between devices, from_behind(): return lax.ppermute(value, axis, pairs)  70.6 us
    ppermute x16, waiting for transfers between devices, from_behind(): return lax.ppermute(value, axis, pairs)  51.6 us
    unnamed x189, local copies, waits for them, and re-layouts  15.2 us
    psum x1, blocking collectives, per_device(): squares = lax.psum(squares, 'chan')  10.2 us
  transfers between devices with their start and end apart: 18, of which 16 were waited for; matrix products, arithmetic and copies ran while one was open for 8% of the time, Pallas kernels for 0%

commit v1 on v0

--- a/solution.py
+++ b/solution.py
@@ -153,7 +153,9 @@
     squares = jnp.sum(mixed * mixed, axis=1)
     scaled = cotangent.astype(jnp.float32) * norm_gain
     dots = jnp.sum(scaled * mixed, axis=1)
-    squares = lax.psum(squares, "chan")
+    squares = squares
+    for hop in (1, 2, 4):
+        squares = squares + lax.ppermute(squares, "chan", [(dev, dev ^ hop) for dev in range(8)])
     model_width = local_width * lax.axis_size("chan")
     inverse = lax.rsqrt(squares / model_width + 1e-06)
     normed = (mixed * inverse[:, None] * norm_gain).astype(jnp.bfloat16)

time: 366 us -> 375 us (1.025)
  starting transfers between devices: 70.7 us -> 79.1 us
    ppermute x0 -> x3, starting transfers between devices: none -> 8.37 us  [per_device(): lax.ppermute(squares, 'chan', [(dev, dev ^ hop) for dev in range(8)])]
    unnamed x189 -> x179, local copies, waits for them, and re-layouts: 15.2 us -> 14 us
  transfers between devices with their start and end apart: 18 -> 21, of which waited for: 16 -> 18; matrix products, arithmetic and copies ran while one was open for 8% -> 8% of each run, Pallas kernels for 0% -> 0%
where the time goes in v1:
time: 375 us; the launch traced here: 374 us
  waiting for transfers between devices  207 us (55%)
  starting transfers between devices  79.1 us (21%)
  local copies, waits for them, and re-layouts  36.4 us (10%)
  other arithmetic  21.6 us (6%)
  between operations  15.8 us (4%)
  blocking collectives  10.6 us (3%)
    psum x2, waiting for transfers between devices, per_device(): packed = lax.psum(lax.psum(packed, 'y'), 'z')  152 us
    ppermute x16, starting transfers between devices, from_behind(): return lax.ppermute(value, axis, pairs)  70.6 us
    ppermute x16, waiting for transfers between devices, from_behind(): return lax.ppermute(value, axis, pairs)  51.6 us
    unnamed x179, local copies, waits for them, and re-layouts  14 us
    psum x1, blocking collectives, per_device(): dots = lax.psum(dots, 'chan')  10.6 us
    ppermute x3, starting transfers between devices, per_device(): lax.ppermute(squares, 'chan', [(dev, dev ^ hop) for dev in range(8)])  8.37 us
  transfers between devices with their start and end apart: 21, of which 18 were waited for; matrix products, arithmetic and copies ran while one was open for 8% of the time, Pallas kernels for 0%

profile of v1, /device:TPU:2, one launch (start us, length us, event | category | flops | bytes accessed | tf_op | source)
XLA Modules:
  0.0 374.0 jit_solution(6204604352598977779)
XLA Ops:
  8.2 3.5 collective-permute-start
  15.0 1.3 fusion.68
  16.3 2.5 multiply_cosine_fusion.1
  21.1 1.1 fusion.18
  27.3 3.5 collective-permute-start.1
  30.8 1.3 collective-permute-done.1
  32.2 4.2 %collective-permute-start.2 = (f32[4,512]{1,0:T(4,128)S(1)}, f32[4,512]{1,0:T(4,128)S(1)}, u32[]{:S(2)}, u32[]{:S(2)}) collective-permute-start(f32[4,512]{1,0:T(4,128)S(1)} %broadcast_select_fusion.5), channel_id=1, source_target_pairs={{0,8},{8,16},{16,24},{24,32},{32,40},{40,48},{48,56},{56,64},{64,7... | collective-permute-start | bytes 24584 | tf_op jit(solution)/shard_map/ppermute | solution.py:12
  36.4 1.3 collective-permute-done.2
  37.8 5.7 %collective-permute-start.3 = (f32[4,512]{1,0:T(4,128)S(1)}, f32[4,512]{1,0:T(4,128)S(1)}, u32[]{:S(2)}, u32[]{:S(2)}) collective-permute-start(f32[4,512]{1,0:T(4,128)S(1)} %maximum_select_fusion), channel_id=1, source_target_pairs={{0,16},{8,24},{16,32},{24,40},{32,48},{40,56},{48,64},{56,72},{64,... | collective-permute-start | bytes 24584 | tf_op jit(solution)/shard_map/ppermute | solution.py:12
  43.5 1.3 collective-permute-done.3
  44.9 10.6 %collective-permute-start.4 = (f32[4,512]{1,0:T(4,128)S(1)}, f32[4,512]{1,0:T(4,128)S(1)}, u32[]{:S(2)}, u32[]{:S(2)}) collective-permute-start(f32[4,512]{1,0:T(4,128)S(1)} %maximum_select_fusion.1), channel_id=1, source_target_pairs={{0,32},{8,40},{16,48},{24,56},{32,64},{40,72},{48,80},{56,88},{64,... | collective-permute-start | bytes 24584 | tf_op jit(solution)/shard_map/ppermute | solution.py:12
  55.5 1.3 collective-permute-done.4
  56.9 9.1 %collective-permute-start.5 = (f32[4,512]{1,0:T(4,128)S(1)}, f32[4,512]{1,0:T(4,128)S(1)}, u32[]{:S(2)}, u32[]{:S(2)}) collective-permute-start(f32[4,512]{1,0:T(4,128)S(1)} %maximum_select_fusion.2), channel_id=1, source_target_pairs={{0,64},{8,72},{16,80},{24,88},{32,96},{40,104},{48,112},{56,120},{... | collective-permute-start | bytes 24584 | tf_op jit(solution)/shard_map/ppermute | solution.py:12
  66.0 1.3 collective-permute-done.5
  67.5 6.1 %collective-permute-start.6 = (f32[4,512]{1,0:T(4,128)S(1)}, f32[4,512]{1,0:T(4,128)S(1)}, u32[]{:S(2)}, u32[]{:S(2)}) collective-permute-start(f32[4,512]{1,0:T(4,128)S(1)} %maximum_select_fusion.3), channel_id=1, source_target_pairs={{0,128},{8,136},{16,144},{24,152},{32,160},{40,168},{48,176},{56,1... | collective-permute-start | bytes 24584 | tf_op jit(solution)/shard_map/ppermute | solution.py:12
  73.6 1.3 collective-permute-done.6
  76.2 17.7 %collective-permute-start.7 = (f32[4,512]{1,0:T(4,128)}, f32[4,512]{1,0:T(4,128)}, u32[]{:S(2)}, u32[]{:S(2)}) collective-permute-start(f32[4,512]{1,0:T(4,128)} %maximum_select_fusion.4), channel_id=1, source_target_pairs={{0,256},{8,264},{16,272},{24,280},{32,288},{40,296},{48,304},{56,3... | collective-permute-start | bytes 24584 | tf_op jit(solution)/shard_map/ppermute | solution.py:12
  96.8 1.1 sub.357
  101.9 1.0 copy.140
  107.1 1.1 squeeze.79
  113.7 2.7 subtract_convert_fusion
  117.9 1.9 collective-permute-start.8
  119.8 1.1 collective-permute-done.8
  120.9 2.4 collective-permute-start.9
  124.2 2.2 collective-permute-done.9
  126.4 4.0 %collective-permute-start.10 = (f32[128]{0:T(128)S(1)}, f32[128]{0:T(128)S(1)}, u32[]{:S(2)}, u32[]{:S(2)}) collective-permute-start(f32[128]{0:T(128)S(1)} %add.435), channel_id=1, source_target_pairs={{0,4},{1,5},{2,6},{3,7},{4,0},{5,1},{6,2},{7,3},{8,12},{9,13},{10,... | collective-permute-start | bytes 1544 | tf_op jit(solution)/shard_map/ppermute | solution.py:158
  130.4 10.6 %psum.35 = f32[128]{0:T(128)S(1)} all-reduce(f32[128]{0:T(128)S(1)} %get-tuple-element.184), channel_id=1, replica_groups=mesh['z'=8,'y'=8,'chan'=8] {'chan'}, use_global_device_ids=true, to_apply=%region_8.9 | all-reduce | flops 128 | bytes 1024 | tf_op jit(solution)/shard_map/psum | solution.py:162
  146.3 1.3 collective-permute-start.11
  147.6 4.2 %collective-permute-done.11 = f32[4,512]{1,0:T(4,128)S(1)} collective-permute-done((f32[4,512]{1,0:T(4,128)S(1)}, f32[4,512]{1,0:T(4,128)S(1)}, u32[]{:S(2)}, u32[]{:S(2)}) %collective-permute-start.11) | collective-permute-done | bytes 8224 | tf_op jit(solution)/shard_map/ppermute | solution.py:12
  151.9 1.3 collective-permute-start.12
  153.2 4.2 %collective-permute-done.12 = f32[4,512]{1,0:T(4,128)S(1)} collective-permute-done((f32[4,512]{1,0:T(4,128)S(1)}, f32[4,512]{1,0:T(4,128)S(1)}, u32[]{:S(2)}, u32[]{:S(2)}) %collective-permute-start.12) | collective-permute-done | bytes 8224 | tf_op jit(solution)/shard_map/ppermute | solution.py:12
  157.5 1.3 collective-permute-start.13
  158.8 5.1 %collective-permute-done.13 = f32[4,512]{1,0:T(4,128)S(1)} collective-permute-done((f32[4,512]{1,0:T(4,128)S(1)}, f32[4,512]{1,0:T(4,128)S(1)}, u32[]{:S(2)}, u32[]{:S(2)}) %collective-permute-start.13) | collective-permute-done | bytes 8224 | tf_op jit(solution)/shard_map/ppermute | solution.py:12
  164.0 1.3 collective-permute-start.14
  165.3 8.1 %collective-permute-done.14 = f32[4,512]{1,0:T(4,128)S(1)} collective-permute-done((f32[4,512]{1,0:T(4,128)S(1)}, f32[4,512]{1,0:T(4,128)S(1)}, u32[]{:S(2)}, u32[]{:S(2)}) %collective-permute-start.14) | collective-permute-done | bytes 8224 | tf_op jit(solution)/shard_map/ppermute | solution.py:12
  173.5 1.3 collective-permute-start.15
  174.8 4.3 %collective-permute-done.15 = f32[4,512]{1,0:T(4,128)S(1)} collective-permute-done((f32[4,512]{1,0:T(4,128)S(1)}, f32[4,512]{1,0:T(4,128)S(1)}, u32[]{:S(2)}, u32[]{:S(2)}) %collective-permute-start.15) | collective-permute-done | bytes 8224 | tf_op jit(solution)/shard_map/ppermute | solution.py:12
  179.1 1.3 collective-permute-start.16
  181.4 4.1 %collective-permute-done.16 = f32[4,512]{1,0:T(4,128)S(1)} collective-permute-done((f32[4,512]{1,0:T(4,128)S(1)}, f32[4,512]{1,0:T(4,128)S(1)}, u32[]{:S(2)}, u32[]{:S(2)}) %collective-permute-start.16) | collective-permute-done | bytes 8224 | tf_op jit(solution)/shard_map/ppermute | solution.py:12
  185.6 1.3 collective-permute-start.17
  186.9 1.0 fusion.35
  187.9 7.2 %collective-permute-done.17 = f32[4,512]{1,0:T(4,128)S(1)} collective-permute-done((f32[4,512]{1,0:T(4,128)S(1)}, f32[4,512]{1,0:T(4,128)S(1)}, u32[]{:S(2)}, u32[]{:S(2)}) %collective-permute-start.17) | collective-permute-done | bytes 8224 | tf_op jit(solution)/shard_map/ppermute | solution.py:12
  195.9 1.1 multiply_subtract_fusion
  201.3 80.8 %all-reduce.5.cloned.1.call-done = (f32[67584]{0:T(1024)}, f32[8,64,128]{2,1,0:T(8,128)}) async-done(((f32[67584]{0:T(1024)}, f32[8,64,128]{2,1,0:T(8,128)}), (f32[67584]{0:T(1024)}, f32[8,64,128]{2,1,0:T(8,128)})) %all-reduce.5.cloned.1.call-update) | async-done | bytes 532496 | tf_op jit(solution)/shard_map/psum | solution.py:221
  282.1 1.3 collective-permute-start.18
  284.2 6.2 %collective-permute-done.18 = f32[3,512]{0,1:T(8,128)S(1)} collective-permute-done((f32[3,512]{0,1:T(8,128)S(1)}, f32[3,512]{0,1:T(8,128)S(1)}, u32[]{:S(2)}, u32[]{:S(2)}) %collective-permute-start.18) | collective-permute-done | bytes 6176 | tf_op jit(solution)/shard_map/ppermute | solution.py:12
  291.9 71.5 %all-reduce.7.cloned.1.call-done = (f32[67584]{0:T(1024)}, f32[8,64,128]{2,1,0:T(8,128)}) async-done(((f32[67584]{0:T(1024)}, f32[8,64,128]{2,1,0:T(8,128)}), (f32[67584]{0:T(1024)}, f32[8,64,128]{2,1,0:T(8,128)})) %all-reduce.7.cloned.1.call-update) | async-done | bytes 532496 | tf_op jit(solution)/shard_map/psum | solution.py:221
  363.4 1.7 slice.228
  (357 shorter events, 47.4 us)
Async XLA Ops:
  7.2 109.3 %copy-start = (bf16[8,64,128]{2,1,0:T(8,128)(2,1)S(1)}, bf16[8,64,128]{2,1,0:T(8,128)(2,1)}, u32[]{:S(2)}) copy-start(bf16[8,64,128]{2,1,0:T(8,128)(2,1)} %param.19) | copy-start | bytes 393220
  7.2 274.9 %all-reduce.5.cloned.1.call-start = ((), (), s32[]{:S(2)}) async-start(), calls=%async_computation | async-start | bytes 1064960 | tf_op jit(solution)/shard_map/psum | solution.py:221
  8.1 3.5 copy-start.84
  8.2 14.0 %collective-permute-start = (bf16[3,512]{0,1:T(8,128)(2,1)S(1)}, bf16[3,512]{0,1:T(8,128)(2,1)S(1)}, u32[]{:S(2)}, u32[]{:S(2)}) collective-permute-start(bf16[3,512]{0,1:T(8,128)(2,1)S(1)} %copy.131), channel_id=1, source_target_pairs={{0,8},{8,16},{16,24},{24,32},{32,40},{40,48},{48,56},{56,64},{64,7... | collective-permute-start | bytes 9224 | tf_op jit(solution)/shard_map/ppermute | solution.py:12
  14.3 4.5 %copy-start.70 = (f32[2,64]{1,0:T(2,128)}, f32[2,64]{1,0:T(2,128)S(1)}, u32[]{:S(2)}) copy-start(f32[2,64]{1,0:T(2,128)S(1)} %reduce.6) | copy-start | bytes 1540
  16.3 8.4 %copy-start.55 = (f32[512]{0:T(512)}, f32[512]{0:T(512)S(1)}, u32[]{:S(2)}) copy-start(f32[512]{0:T(512)S(1)} %get-tuple-element.356) | copy-start | bytes 6148
  16.3 11.0 %copy-start.57 = (f32[512]{0:T(512)}, f32[512]{0:T(512)S(1)}, u32[]{:S(2)}) copy-start(f32[512]{0:T(512)S(1)} %get-tuple-element.352) | copy-start | bytes 6148
  20.3 2.0 copy-start.47
  20.3 2.0 copy-start.49
  20.4 2.0 copy-start.51
  20.4 2.0 copy-start.53
  27.3 4.8 %collective-permute-start.1 = (f32[4,512]{1,0:T(4,128)S(1)}, f32[4,512]{1,0:T(4,128)S(1)}, u32[]{:S(2)}, u32[]{:S(2)}) collective-permute-start(f32[4,512]{1,0:T(4,128)S(1)} %fusion.48), channel_id=1, source_target_pairs={{0,8},{8,16},{16,24},{24,32},{32,40},{40,48},{48,56},{56,64},{64,7... | collective-permute-start | bytes 24584 | tf_op jit(solution)/shard_map/ppermute | solution.py:12
  32.2 5.5 %collective-permute-start.2 = (f32[4,512]{1,0:T(4,128)S(1)}, f32[4,512]{1,0:T(4,128)S(1)}, u32[]{:S(2)}, u32[]{:S(2)}) collective-permute-start(f32[4,512]{1,0:T(4,128)S(1)} %broadcast_select_fusion.5), channel_id=1, source_target_pairs={{0,8},{8,16},{16,24},{24,32},{32,40},{40,48},{48,56},{56,64},{64,7... | collective-permute-start | bytes 24584 | tf_op jit(solution)/shard_map/ppermute | solution.py:12
  37.8 7.1 %collective-permute-start.3 = (f32[4,512]{1,0:T(4,128)S(1)}, f32[4,512]{1,0:T(4,128)S(1)}, u32[]{:S(2)}, u32[]{:S(2)}) collective-permute-start(f32[4,512]{1,0:T(4,128)S(1)} %maximum_select_fusion), channel_id=1, source_target_pairs={{0,16},{8,24},{16,32},{24,40},{32,48},{40,56},{48,64},{56,72},{64,... | collective-permute-start | bytes 24584 | tf_op jit(solution)/shard_map/ppermute | solution.py:12
  44.8 30.2 %copy-start.17 = (f32[1,512]{1,0:T(1,128)}, f32[1,512]{1,0:T(1,128)S(1)}, u32[]{:S(2)}) copy-start(f32[1,512]{1,0:T(1,128)S(1)} %get-tuple-element.319) | copy-start | bytes 6148
  44.8 30.2 %copy-start.19 = (f32[1,512]{1,0:T(1,128)}, f32[1,512]{1,0:T(1,128)S(1)}, u32[]{:S(2)}) copy-start(f32[1,512]{1,0:T(1,128)S(1)} %get-tuple-element.320) | copy-start | bytes 6148
  44.9 30.2 %copy-start.21 = (f32[1,512]{1,0:T(1,128)}, f32[1,512]{1,0:T(1,128)S(1)}, u32[]{:S(2)}) copy-start(f32[1,512]{1,0:T(1,128)S(1)} %get-tuple-element.321) | copy-start | bytes 6148
  44.9 30.2 %copy-start.23 = (f32[1,512]{1,0:T(1,128)}, f32[1,512]{1,0:T(1,128)S(1)}, u32[]{:S(2)}) copy-start(f32[1,512]{1,0:T(1,128)S(1)} %get-tuple-element.322) | copy-start | bytes 6148
  44.9 11.9 %collective-permute-start.4 = (f32[4,512]{1,0:T(4,128)S(1)}, f32[4,512]{1,0:T(4,128)S(1)}, u32[]{:S(2)}, u32[]{:S(2)}) collective-permute-start(f32[4,512]{1,0:T(4,128)S(1)} %maximum_select_fusion.1), channel_id=1, source_target_pairs={{0,32},{8,40},{16,48},{24,56},{32,64},{40,72},{48,80},{56,88},{64,... | collective-permute-start | bytes 24584 | tf_op jit(solution)/shard_map/ppermute | solution.py:12
  56.8 18.2 %copy-start.27 = (f32[1,512]{1,0:T(1,128)}, f32[1,512]{1,0:T(1,128)S(1)}, u32[]{:S(2)}) copy-start(f32[1,512]{1,0:T(1,128)S(1)} %get-tuple-element.315) | copy-start | bytes 6148
  56.8 18.2 %copy-start.29 = (f32[1,512]{1,0:T(1,128)}, f32[1,512]{1,0:T(1,128)S(1)}, u32[]{:S(2)}) copy-start(f32[1,512]{1,0:T(1,128)S(1)} %get-tuple-element.316) | copy-start | bytes 6148
  56.9 18.2 %copy-start.31 = (f32[1,512]{1,0:T(1,128)}, f32[1,512]{1,0:T(1,128)S(1)}, u32[]{:S(2)}) copy-start(f32[1,512]{1,0:T(1,128)S(1)} %get-tuple-element.317) | copy-start | bytes 6148
  56.9 18.2 %copy-start.33 = (f32[1,512]{1,0:T(1,128)}, f32[1,512]{1,0:T(1,128)S(1)}, u32[]{:S(2)}) copy-start(f32[1,512]{1,0:T(1,128)S(1)} %get-tuple-element.318) | copy-start | bytes 6148
  56.9 10.5 %collective-permute-start.5 = (f32[4,512]{1,0:T(4,128)S(1)}, f32[4,512]{1,0:T(4,128)S(1)}, u32[]{:S(2)}, u32[]{:S(2)}) collective-permute-start(f32[4,512]{1,0:T(4,128)S(1)} %maximum_select_fusion.2), channel_id=1, source_target_pairs={{0,64},{8,72},{16,80},{24,88},{32,96},{40,104},{48,112},{56,120},{... | collective-permute-start | bytes 24584 | tf_op jit(solution)/shard_map/ppermute | solution.py:12
  67.4 7.7 %copy-start.39 = (f32[1,512]{1,0:T(1,128)}, f32[1,512]{1,0:T(1,128)S(1)}, u32[]{:S(2)}) copy-start(f32[1,512]{1,0:T(1,128)S(1)} %get-tuple-element.311) | copy-start | bytes 6148
  67.4 7.7 %copy-start.41 = (f32[1,512]{1,0:T(1,128)}, f32[1,512]{1,0:T(1,128)S(1)}, u32[]{:S(2)}) copy-start(f32[1,512]{1,0:T(1,128)S(1)} %get-tuple-element.312) | copy-start | bytes 6148
  67.4 7.7 %copy-start.43 = (f32[1,512]{1,0:T(1,128)}, f32[1,512]{1,0:T(1,128)S(1)}, u32[]{:S(2)}) copy-start(f32[1,512]{1,0:T(1,128)S(1)} %get-tuple-element.313) | copy-start | bytes 6148
  67.4 7.7 %copy-start.45 = (f32[1,512]{1,0:T(1,128)}, f32[1,512]{1,0:T(1,128)S(1)}, u32[]{:S(2)}) copy-start(f32[1,512]{1,0:T(1,128)S(1)} %get-tuple-element.314) | copy-start | bytes 6148
  67.5 7.4 %collective-permute-start.6 = (f32[4,512]{1,0:T(4,128)S(1)}, f32[4,512]{1,0:T(4,128)S(1)}, u32[]{:S(2)}, u32[]{:S(2)}) collective-permute-start(f32[4,512]{1,0:T(4,128)S(1)} %maximum_select_fusion.3), channel_id=1, source_target_pairs={{0,128},{8,136},{16,144},{24,152},{32,160},{40,168},{48,176},{56,1... | collective-permute-start | bytes 24584 | tf_op jit(solution)/shard_map/ppermute | solution.py:12
  76.2 34.9 %collective-permute-start.7 = (f32[4,512]{1,0:T(4,128)}, f32[4,512]{1,0:T(4,128)}, u32[]{:S(2)}, u32[]{:S(2)}) collective-permute-start(f32[4,512]{1,0:T(4,128)} %maximum_select_fusion.4), channel_id=1, source_target_pairs={{0,256},{8,264},{16,272},{24,280},{32,288},{40,296},{48,304},{56,3... | collective-permute-start | bytes 24584 | tf_op jit(solution)/shard_map/ppermute | solution.py:12
  110.0 2.2 copy-start.66
  110.9 2.2 copy-start.6
  110.9 2.2 copy-start.7
  110.9 2.2 copy-start.8
  117.9 3.1 collective-permute-start.8
  120.9 5.5 %collective-permute-start.9 = (f32[128]{0:T(128)S(1)}, f32[128]{0:T(128)S(1)}, u32[]{:S(2)}, u32[]{:S(2)}) collective-permute-start(f32[128]{0:T(128)S(1)} %add.434), channel_id=1, source_target_pairs={{0,2},{1,3},{2,0},{3,1},{4,6},{5,7},{6,4},{7,5},{8,10},{9,11},{10,... | collective-permute-start | bytes 1544 | tf_op jit(solution)/shard_map/ppermute | solution.py:158
  126.4 14.6 %collective-permute-start.10 = (f32[128]{0:T(128)S(1)}, f32[128]{0:T(128)S(1)}, u32[]{:S(2)}, u32[]{:S(2)}) collective-permute-start(f32[128]{0:T(128)S(1)} %add.435), channel_id=1, source_target_pairs={{0,4},{1,5},{2,6},{3,7},{4,0},{5,1},{6,2},{7,3},{8,12},{9,13},{10,... | collective-permute-start | bytes 1544 | tf_op jit(solution)/shard_map/ppermute | solution.py:158
  142.6 2.0 copy-start.11
  146.3 5.5 %collective-permute-start.11 = (f32[4,512]{1,0:T(4,128)S(1)}, f32[4,512]{1,0:T(4,128)S(1)}, u32[]{:S(2)}, u32[]{:S(2)}) collective-permute-start(f32[4,512]{1,0:T(4,128)S(1)} %fusion.50), channel_id=1, source_target_pairs={{8,0},{16,8},{24,16},{32,24},{40,32},{48,40},{56,48},{64,56},{72,6... | collective-permute-start | bytes 24584 | tf_op jit(solution)/shard_map/ppermute | solution.py:12
  151.9 5.5 %collective-permute-start.12 = (f32[4,512]{1,0:T(4,128)S(1)}, f32[4,512]{1,0:T(4,128)S(1)}, u32[]{:S(2)}, u32[]{:S(2)}) collective-permute-start(f32[4,512]{1,0:T(4,128)S(1)} %broadcast_select_fusion.4), channel_id=1, source_target_pairs={{8,0},{16,8},{24,16},{32,24},{40,32},{48,40},{56,48},{64,56},{72,6... | collective-permute-start | bytes 24584 | tf_op jit(solution)/shard_map/ppermute | solution.py:12
  157.5 6.4 %collective-permute-start.13 = (f32[4,512]{1,0:T(4,128)S(1)}, f32[4,512]{1,0:T(4,128)S(1)}, u32[]{:S(2)}, u32[]{:S(2)}) collective-permute-start(f32[4,512]{1,0:T(4,128)S(1)} %maximum_select_fusion.6), channel_id=1, source_target_pairs={{16,0},{24,8},{32,16},{40,24},{48,32},{56,40},{64,48},{72,56},{80,... | collective-permute-start | bytes 24584 | tf_op jit(solution)/shard_map/ppermute | solution.py:12
  164.0 9.5 %collective-permute-start.14 = (f32[4,512]{1,0:T(4,128)S(1)}, f32[4,512]{1,0:T(4,128)S(1)}, u32[]{:S(2)}, u32[]{:S(2)}) collective-permute-start(f32[4,512]{1,0:T(4,128)S(1)} %maximum_select_fusion.7), channel_id=1, source_target_pairs={{32,0},{40,8},{48,16},{56,24},{64,32},{72,40},{80,48},{88,56},{96,... | collective-permute-start | bytes 24584 | tf_op jit(solution)/shard_map/ppermute | solution.py:12
  173.5 5.6 %collective-permute-start.15 = (f32[4,512]{1,0:T(4,128)S(1)}, f32[4,512]{1,0:T(4,128)S(1)}, u32[]{:S(2)}, u32[]{:S(2)}) collective-permute-start(f32[4,512]{1,0:T(4,128)S(1)} %maximum_select_fusion.8), channel_id=1, source_target_pairs={{64,0},{72,8},{80,16},{88,24},{96,32},{104,40},{112,48},{120,56},{... | collective-permute-start | bytes 24584 | tf_op jit(solution)/shard_map/ppermute | solution.py:12
  179.1 6.4 %collective-permute-start.16 = (f32[4,512]{1,0:T(4,128)S(1)}, f32[4,512]{1,0:T(4,128)S(1)}, u32[]{:S(2)}, u32[]{:S(2)}) collective-permute-start(f32[4,512]{1,0:T(4,128)S(1)} %maximum_select_fusion.9), channel_id=1, source_target_pairs={{128,0},{136,8},{144,16},{152,24},{160,32},{168,40},{176,48},{184,... | collective-permute-start | bytes 24584 | tf_op jit(solution)/shard_map/ppermute | solution.py:12
  185.6 9.5 %collective-permute-start.17 = (f32[4,512]{1,0:T(4,128)S(1)}, f32[4,512]{1,0:T(4,128)S(1)}, u32[]{:S(2)}, u32[]{:S(2)}) collective-permute-start(f32[4,512]{1,0:T(4,128)S(1)} %maximum_select_fusion.10), channel_id=1, source_target_pairs={{256,0},{264,8},{272,16},{280,24},{288,32},{296,40},{304,48},{312,... | collective-permute-start | bytes 24584 | tf_op jit(solution)/shard_map/ppermute | solution.py:12
  201.2 162.2 %all-reduce.7.cloned.1.call-start = ((), (), s32[]{:S(2)}) async-start(), calls=%async_computation.1 | async-start | bytes 1064960 | tf_op jit(solution)/shard_map/psum | solution.py:221
  282.1 8.3 %collective-permute-start.18 = (f32[3,512]{0,1:T(8,128)S(1)}, f32[3,512]{0,1:T(8,128)S(1)}, u32[]{:S(2)}, u32[]{:S(2)}) collective-permute-start(f32[3,512]{0,1:T(8,128)S(1)} %bitcast.248), channel_id=1, source_target_pairs={{8,0},{16,8},{24,16},{32,24},{40,32},{48,40},{56,48},{64,56},{72,6... | collective-permute-start | bytes 18440 | tf_op jit(solution)/shard_map/ppermute | solution.py:12
  363.4 3.0 copy-start.13
  (58 other events, 49.2 us)
Sparse Core Ops, SparseCore 0:
  201.4 80.6 all-reduce.4
  284.5 78.8 all-reduce.6
